TPU v7x, 32 devices: a whole 2x2x4 slice. The times are simulated.
32 devices in a mesh: seq: 4 (over z), tp: 4 (over y, x), dp: 2 (over core).
Axes of the slice: x: 2, y: 2, z: 4, core: 2. Of those that a mesh axis runs over, the one named last changes fastest.
Arguments:
- hidden_states: bfloat16 [2048, 7168], P(('dp', 'seq'), 'tp'), parts along dimension 0, may hold values from -120 to 120
- input_gain: float32 [7168], P('tp'), may hold values from 0.1 to 1.9
- query_down: bfloat16 [7168, 1536], P('tp', 'seq'), may hold values from -0.0625 to 0.0625
- memory_down: bfloat16 [7168, 576], P('tp', 'seq'), may hold values from -0.0625 to 0.0625
- query_gain: float32 [1536], replicated, may hold values from 0.1 to 1.9
- memory_gain: float32 [512], replicated, may hold values from 0.1 to 1.9
- query_up: bfloat16 [1536, 12288], P('seq', 'tp'), may hold values from -16 to 16
- key_up: bfloat16 [512, 8192], P('seq', 'tp'), may hold values from -0.25 to 0.25
- value_up: bfloat16 [512, 8192], P('seq', 'tp'), may hold values from -0.25 to 0.25
- segment_ids: int32 [2048], P(('dp', 'seq')), parts along dimension 0, may hold values from 0 to 11, never falling along the last dimension, each value on 1 to 256 neighbouring positions
Outputs:
- attended: bfloat16 [2048, 8192], P(('dp', 'seq'), 'tp'), parts along dimension 0
There are 2 independent parts, one for each index of `dp`. A program takes and returns all parts, laid end to end along the dimension named above; an argument that names none is the same for every part. Nothing has to cross between parts.
Inputs may be any that keep to these rules, and one draw needn't show every extreme that they name: `segment_ids`: ids never fall along the group; each of the 12 documents has 1 to 256 tokens and one has exactly 256.
All inputs are finite; a program needn't handle non-finite values.
Results may differ from a plain program's by a relative error of at most 0.0065.
The roundings to bfloat16 on the way count: a program that leaves them out, or rounds other values in their place, can miss the bound.
Values may be sent and summed in bfloat16 or wider, within the bound.
No kernel may reach another device: no remote copies, remote signals or barrier semaphores. Data moves between devices by JAX's collectives and lax.ppermute only.
A program may use at most 128 MiB of HBM per device.

v0:
```python
import jax
import jax.numpy as jnp
from jax import lax
from jax.sharding import PartitionSpec as P

KVRANK = 512
NOPE = 128
ROPE = 64
VDIM = 128
DOCS = 12
epsilon = 1e-06


def rms_scale(entries, gain_vector):
    return (
        entries * lax.rsqrt(jnp.mean(entries * entries, -1, keepdims=True) + epsilon) * gain_vector
    )


def rotate(entries, position):
    half_width = entries.shape[-1] // 2
    frequency = jnp.power(10000.0, -2.0 * jnp.arange(half_width, dtype=jnp.float32) / ROPE)
    angles = position.astype(jnp.float32)[..., None] * frequency
    cosine = jnp.cos(angles)
    sine_part = jnp.sin(angles)
    first_half = entries[..., :half_width]
    second_half = entries[..., half_width:]
    return jnp.concatenate(
        [
            first_half * cosine - second_half * sine_part,
            second_half * cosine + first_half * sine_part,
        ],
        -1,
    )


def heads_attention(query_all, key_all, value_all, group_ids, score_scale, doc_most):
    total_rows = query_all.shape[0]
    block_rows = min(512, total_rows)
    key_index = jnp.arange(total_rows, dtype=jnp.int32)
    results = []
    for block in range(total_rows // block_rows):
        lower = block * block_rows
        upper = lower + block_rows
        key_low = max(0, lower - doc_most)
        scores = (
            jnp.einsum(
                "qhd,khd->hqk",
                query_all[lower:upper],
                key_all[key_low:upper],
                preferred_element_type=jnp.float32,
            )
            * score_scale
        )
        allowed = (group_ids[lower:upper, None] == group_ids[None, key_low:upper]) & (
            key_index[lower:upper, None] >= key_index[None, key_low:upper]
        )
        scores = jnp.where(allowed[None], scores, -jnp.inf)
        row_max = jnp.max(scores, -1, keepdims=True)
        probs_full = jnp.exp(scores - row_max)
        denominator = jnp.sum(probs_full, -1)
        weights = probs_full.astype(jnp.bfloat16)
        weighted = jnp.einsum(
            "hqk,khd->qhd", weights, value_all[key_low:upper], preferred_element_type=jnp.float32
        )
        results.append((weighted / jnp.transpose(denominator)[:, :, None]).astype(jnp.bfloat16))
    return jnp.concatenate(results, 0)


def body(
    hidden_states,
    input_gain,
    query_down,
    memory_down,
    query_gain,
    memory_gain,
    query_up,
    key_up,
    value_up,
    segment_ids,
):
    tok_count = hidden_states.shape[0]
    seq_count = lax.axis_size("seq")
    tp_count = lax.axis_size("tp")
    seq_index = lax.axis_index("seq")
    tp_index = lax.axis_index("tp")
    width = hidden_states.shape[1] * tp_count
    total_rows = tok_count * seq_count
    doc_most = total_rows // 4
    qrank_piece = query_down.shape[1]
    memory_piece = memory_down.shape[1]
    qrank = qrank_piece * seq_count
    memory_cols = memory_piece * seq_count
    group_ids = lax.all_gather(segment_ids, "seq", axis=0, tiled=True)
    token_index = jnp.arange(total_rows, dtype=jnp.int32)
    onehot = group_ids[:, None] == jnp.arange(DOCS, dtype=jnp.int32)[None, :]
    starts = jnp.min(jnp.where(onehot, token_index[:, None], total_rows), 0)
    position = token_index - jnp.sum(jnp.where(onehot, starts[None, :], 0), 1)
    inputs = hidden_states.astype(jnp.float32)
    square_sums = lax.psum(jnp.sum(inputs * inputs, 1), "tp")
    normed = (inputs * lax.rsqrt(square_sums / width + epsilon)[:, None] * input_gain).astype(
        jnp.bfloat16
    )
    down_piece = jnp.concatenate([query_down, memory_down], 1)
    down_all = lax.all_gather(down_piece, "seq", axis=1, tiled=True)
    partial = jnp.dot(normed, down_all, preferred_element_type=jnp.float32)
    latent_rows = lax.psum_scatter(partial, "tp", scatter_dimension=0, tiled=True)
    chunk = latent_rows.shape[0]
    latent_rows = latent_rows.reshape(chunk, seq_count, qrank_piece + memory_piece)
    query_sums = latent_rows[:, :, :qrank_piece].reshape(chunk, qrank)
    memory_sums = latent_rows[:, :, qrank_piece:].reshape(chunk, memory_cols)
    chunk_position = lax.dynamic_slice(
        position, (seq_index * tok_count + tp_index * chunk,), (chunk,)
    )
    compressed_query = rms_scale(query_sums, query_gain).astype(jnp.bfloat16)
    compressed_memory = rms_scale(memory_sums[:, :KVRANK], memory_gain).astype(jnp.bfloat16)
    key_rope = rotate(memory_sums[:, KVRANK:], chunk_position).astype(jnp.bfloat16)
    packed = jnp.concatenate([compressed_query, compressed_memory, key_rope], 1)
    packed = lax.all_gather(packed, "seq", axis=0, tiled=False)
    packed = lax.all_gather(packed, "tp", axis=0, tiled=False)
    latent = jnp.transpose(packed, (1, 0, 2, 3)).reshape(total_rows, packed.shape[-1])
    cq_all = latent[:, :qrank]
    cm_all = latent[:, qrank : qrank + KVRANK]
    rope_all = latent[:, qrank + KVRANK :]
    local_heads = query_up.shape[1] // (NOPE + ROPE)
    heads = local_heads // seq_count
    query_w = lax.all_to_all(
        query_up.reshape(query_up.shape[0], seq_count, heads * (NOPE + ROPE)),
        "seq",
        split_axis=1,
        concat_axis=0,
        tiled=True,
    ).reshape(qrank, heads * (NOPE + ROPE))
    key_w = lax.all_to_all(
        key_up.reshape(key_up.shape[0], seq_count, heads * NOPE),
        "seq",
        split_axis=1,
        concat_axis=0,
        tiled=True,
    ).reshape(KVRANK, heads * NOPE)
    value_w = lax.all_to_all(
        value_up.reshape(value_up.shape[0], seq_count, heads * VDIM),
        "seq",
        split_axis=1,
        concat_axis=0,
        tiled=True,
    ).reshape(KVRANK, heads * VDIM)
    query_full = jnp.dot(cq_all, query_w, preferred_element_type=jnp.float32).reshape(
        total_rows, heads, NOPE + ROPE
    )
    query = jnp.concatenate(
        [query_full[..., :NOPE], rotate(query_full[..., NOPE:], position[:, None])], -1
    ).astype(jnp.bfloat16)
    key_nope = (
        jnp.dot(cm_all, key_w, preferred_element_type=jnp.float32)
        .astype(jnp.bfloat16)
        .reshape(total_rows, heads, NOPE)
    )
    value = (
        jnp.dot(cm_all, value_w, preferred_element_type=jnp.float32)
        .astype(jnp.bfloat16)
        .reshape(total_rows, heads, VDIM)
    )
    key_all = jnp.concatenate(
        [key_nope, jnp.broadcast_to(rope_all[:, None, :], (total_rows, heads, ROPE))], -1
    )
    score_scale = (NOPE + ROPE) ** (-0.5)
    head_output = heads_attention(query, key_all, value, group_ids, score_scale, doc_most)
    attended = lax.all_to_all(head_output, "seq", split_axis=0, concat_axis=1, tiled=True)
    return attended.reshape(tok_count, local_heads * VDIM)


def solution(mesh):
    in_specs = (
        P(("dp", "seq"), "tp"),
        P("tp"),
        P("tp", "seq"),
        P("tp", "seq"),
        P(),
        P(),
        P("seq", "tp"),
        P("seq", "tp"),
        P("seq", "tp"),
        P(("dp", "seq")),
    )
    out_specs = P(("dp", "seq"), "tp")
    return jax.shard_map(body, mesh=mesh, in_specs=in_specs, out_specs=out_specs, check_vma=False)
```

profile of v0, /device:TPU:0, one launch (start us, length us, event | category | flops | bytes accessed | tf_op | source)
XLA Modules:
  0.0 378.8 jit_solution(2457869246093978417)
XLA Ops:
  6.5 1.8 copy.69
  8.4 2.6 pad_maximum_fusion
  11.3 11.4 %psum.7 = f32[256]{0:T(256)S(1)} all-reduce(f32[256]{0:T(256)S(1)} %fusion.16), channel_id=1, replica_groups=mesh['seq'=4,'tp'=4,'dp'=2] {'tp'}, use_global_device_ids=true, to_apply=%region_1.2 | all-reduce | flops 256 | bytes 2048 | tf_op jit(solution)/shard_map/psum | solution.py:100
  22.7 127.4 %all-gather.7.cloned.1.call-done = bf16[1792,2112]{0,1:T(8,128)(2,1)} async-done(((bf16[1792,528]{0,1:T(8,128)(2,1)}), bf16[1792,2112]{0,1:T(8,128)(2,1)}) %all-gather.7.cloned.1.call-update) | async-done | bytes 7569424 | tf_op jit(solution)/shard_map/all_gather | solution.py:105
  150.1 6.9 %fusion.33 = f32[256,2112]{1,0:T(8,128)} fusion(bf16[1792,2112]{0,1:T(8,128)(2,1)} %all-gather.7.cloned.1.call-done, bf16[256,1792]{1,0:T(8,128)(2,1)S(1)} %copy-done.5, f32[1792]{0:T(1024)S(1)} %copy-done.14, f32[256]{0:T(256)S(1)} %add_rsqrt_fusion), kind=kOutput, calls=%fused_computation.43 | convolution fusion | flops 1939603456 | bytes 10657792 | tf_op jit(solution)/shard_map/dot_general | solution.py:106
  157.1 7.9 %all-gather.2 = s32[4,1,256]{2,1,0:T(1,128)S(1)} all-gather(s32[1,1,256]{2,1,0:T(1,128)S(1)} %bitcast.83), channel_id=1, replica_groups=mesh['seq'=4,'tp'=4,'dp'=2] {'seq'}, dimensions={0}, use_global_device_ids=true | all-gather | bytes 5120 | tf_op jit(solution)/shard_map/all_gather | solution.py:94
  165.3 26.4 %reduce-scatter.2.cloned.1.call-done = f32[64,2112]{1,0:T(8,128)} async-done(((f32[256,2112]{1,0:T(8,128)}), f32[64,2112]{1,0:T(8,128)}) %reduce-scatter.2.cloned.1.call-update) | async-done | bytes 540688 | tf_op jit(solution)/shard_map/reduce_scatter | solution.py:107
  191.7 1.5 reshape.261
  195.7 29.2 %all-gather.9.cloned.1.call-done = bf16[256,2112]{1,0:T(8,128)(2,1)} async-done(((bf16[64,2112]{1,0:T(8,128)(2,1)}), bf16[256,2112]{1,0:T(8,128)(2,1)}) %all-gather.9.cloned.1.call-update) | async-done | bytes 1081360 | tf_op jit(solution)/shard_map/all_gather | solution.py:119
  225.9 3.5 all-to-all-start.2
  230.4 13.3 %all-to-all-done.2 = bf16[128,4,512]{0,2,1:T(8,128)(2,1)S(1)} async-done(((bf16[128,4,512]{0,2,1:T(8,128)(2,1)}), bf16[128,4,512]{0,2,1:T(8,128)(2,1)S(1)}, u32[]{:S(2)}, u32[]{:S(2)}) %all-to-all-start.2) | async-done | bytes 524320 | tf_op jit(solution)/shard_map/all_to_all | solution.py:134
  243.7 3.5 all-to-all-start
  247.1 3.0 copy.77
  250.2 2.7 copy.78
  252.8 8.3 %all-to-all-done = bf16[128,4,512]{0,2,1:T(8,128)(2,1)S(1)} async-done(((bf16[128,4,512]{0,2,1:T(8,128)(2,1)}), bf16[128,4,512]{0,2,1:T(8,128)(2,1)S(1)}, u32[]{:S(2)}, u32[]{:S(2)}) %all-to-all-start) | async-done | bytes 524320 | tf_op jit(solution)/shard_map/all_to_all | solution.py:141
  261.2 3.8 %all-to-all-start.1 = ((bf16[384,4,768]{2,0,1:T(8,128)(2,1)}), bf16[384,4,768]{2,0,1:T(8,128)(2,1)S(1)}, u32[]{:S(2)}, u32[]{:S(2)}) async-start(bf16[384,4,768]{2,0,1:T(8,128)(2,1)} %copy.78), calls=%async_computation.2 | async-start | bytes 4718592 | tf_op jit(solution)/shard_map/all_to_all | solution.py:127
  265.6 1.8 multiply_cosine_fusion
  268.4 1.8 compare_and_fusion
  270.3 1.0 copy.81
  271.5 46.6 %all-to-all-done.1 = bf16[384,4,768]{2,0,1:T(8,128)(2,1)S(1)} async-done(((bf16[384,4,768]{2,0,1:T(8,128)(2,1)}), bf16[384,4,768]{2,0,1:T(8,128)(2,1)S(1)}, u32[]{:S(2)}, u32[]{:S(2)}) %all-to-all-start.1) | async-done | bytes 2359328 | tf_op jit(solution)/shard_map/all_to_all | solution.py:127
  318.1 2.4 copy.79
  320.6 2.6 copy.74
  324.9 2.6 fusion.6
  327.7 1.5 copy-done.3
  329.1 1.8 convolution_convert_fusion
  331.1 1.4 subtract_convert_fusion
  333.8 1.7 fusion
  336.6 1.3 divide_convert_fusion.1
  337.9 1.7 fusion.1
  339.6 2.1 divide_convert_fusion
  342.6 27.7 %all_to_all.60 = bf16[1024,4,128]{2,1,0:T(4,128)(2,1)S(1)} all-to-all(bf16[1024,4,128]{2,1,0:T(4,128)(2,1)S(1)} %copy.84), channel_id=1, replica_groups=mesh['seq'=4,'tp'=4,'dp'=2] {'seq'}, dimensions={0} | all-to-all | bytes 2097152 | tf_op jit(solution)/shard_map/all_to_all | solution.py:169
  370.6 1.6 reshape.272
  (88 shorter events, 12.5 us)
Async XLA Ops:
  6.5 143.5 %all-gather.7.cloned.1.call-start = ((), (), s32[]{:S(2)}) async-start(), calls=%async_computation.5 | async-start | bytes 9461760 | tf_op jit(solution)/shard_map/all_gather | solution.py:105
  8.3 2.7 copy-start.5
  8.4 141.7 %copy-start.14 = (f32[1792]{0:T(1024)S(1)}, f32[1792]{0:T(1024)}, u32[]{:S(2)}) copy-start(f32[1792]{0:T(1024)} %param.11) | copy-start | bytes 21508
  11.0 180.7 %reduce-scatter.2.cloned.1.call-start = ((), (), s32[]{:S(2)}) async-start(), calls=%async_computation.6 | async-start | bytes 2785280 | tf_op jit(solution)/shard_map/reduce_scatter | solution.py:107
  22.7 134.4 %copy-start.13 = (s32[256]{0:T(256)S(1)}, s32[256]{0:T(256)}, u32[]{:S(2)}) copy-start(s32[256]{0:T(256)} %param.19) | copy-start | bytes 3076
  157.0 37.4 %copy-start.11 = (f32[512]{0:T(512)S(1)}, f32[512]{0:T(512)}, u32[]{:S(2)}) copy-start(f32[512]{0:T(512)} %param.15) | copy-start | bytes 6148
  157.0 37.7 %copy-start.10 = (f32[1536]{0:T(1024)S(1)}, f32[1536]{0:T(1024)}, u32[]{:S(2)}) copy-start(f32[1536]{0:T(1024)} %param.14) | copy-start | bytes 18436
  157.0 67.8 %all-gather.9.cloned.1.call-start = ((), (), s32[]{:S(2)}) async-start(), calls=%async_computation.7 | async-start | bytes 1392640 | tf_op jit(solution)/shard_map/all_gather | solution.py:119
  165.0 30.7 %copy-start.12 = (f32[32]{0:T(128)}, f32[32]{0:T(128)S(1)}, u32[]{:S(2)}) copy-start(f32[32]{0:T(128)S(1)} %multiply_power_fusion) | copy-start | bytes 388
  193.2 31.8 %copy-start.7 = (bf16[128,2048]{1,0:T(8,128)(2,1)S(1)}, bf16[128,2048]{1,0:T(8,128)(2,1)}, u32[]{:S(2)}) copy-start(bf16[128,2048]{1,0:T(8,128)(2,1)} %param.17) | copy-start | bytes 1572868
  194.0 35.4 %copy-start.8 = (bf16[128,2048]{1,0:T(8,128)(2,1)S(1)}, bf16[128,2048]{1,0:T(8,128)(2,1)}, u32[]{:S(2)}) copy-start(bf16[128,2048]{1,0:T(8,128)(2,1)} %param.18) | copy-start | bytes 1572868
  195.7 124.9 %all-gather.11.cloned.1.call-start = ((), (), s32[]{:S(2)}) async-start(), calls=%async_computation.8 | async-start | bytes 5570560 | tf_op jit(solution)/shard_map/all_gather | solution.py:120
  225.9 17.7 %all-to-all-start.2 = ((bf16[128,4,512]{0,2,1:T(8,128)(2,1)}), bf16[128,4,512]{0,2,1:T(8,128)(2,1)S(1)}, u32[]{:S(2)}, u32[]{:S(2)}) async-start(bf16[128,4,512]{0,2,1:T(8,128)(2,1)} %bitcast.20), calls=%async_computation.3 | async-start | bytes 1048576 | tf_op jit(solution)/shard_map/all_to_all | solution.py:134
  243.7 17.5 %all-to-all-start = ((bf16[128,4,512]{0,2,1:T(8,128)(2,1)}), bf16[128,4,512]{0,2,1:T(8,128)(2,1)S(1)}, u32[]{:S(2)}, u32[]{:S(2)}) async-start(bf16[128,4,512]{0,2,1:T(8,128)(2,1)} %bitcast.7), calls=%async_computation.1 | async-start | bytes 1048576 | tf_op jit(solution)/shard_map/all_to_all | solution.py:141
  261.2 57.0 %all-to-all-start.1 = ((bf16[384,4,768]{2,0,1:T(8,128)(2,1)}), bf16[384,4,768]{2,0,1:T(8,128)(2,1)S(1)}, u32[]{:S(2)}, u32[]{:S(2)}) async-start(bf16[384,4,768]{2,0,1:T(8,128)(2,1)} %copy.78), calls=%async_computation.2 | async-start | bytes 4718592 | tf_op jit(solution)/shard_map/all_to_all | solution.py:127
  323.2 1.7 copy-start
  324.0 3.5 copy-start.1
  324.9 4.3 %copy-start.9 = (bf16[4,128,1,512]{3,1,0,2:T(8,128)(2,1)S(1)}, bf16[4,128,1,512]{3,1,0,2:T(8,128)(2,1)}, u32[]{:S(2)}) copy-start(bf16[4,128,1,512]{3,1,0,2:T(8,128)(2,1)} %copy.81) | copy-start | bytes 1572868
  327.5 1.6 copy-start.3
  327.5 3.5 copy-start.6
  330.9 1.8 copy-start.4
  331.0 1.7 copy-start.15
  332.8 1.0 copy-start.2
  335.5 1.0 slice-start
  337.9 1.7 slice-start.1
Sparse Core Ops, SparseCore 0:
  11.1 138.9 all-gather.6
  157.2 34.4 reduce-scatter.1
  195.8 29.0 all-gather.8
  226.6 54.1 all-gather.10
where the time goes:
time: 380 us; the launch traced here: 379 us
  waiting for transfers between devices  251 us (66%)
  blocking collectives  46.9 us (12%)
  local copies, waits for them, and re-layouts  24.8 us (7%)
  matrix products  18.2 us (5%)
  between operations  13.6 us (4%)
  other arithmetic  13.2 us (3%)
  starting transfers between devices  10.9 us (3%)
    all_gather x1, waiting for transfers between devices, body(): down_all = lax.all_gather(down_piece, 'seq', axis=1, tiled=True)  127 us
    all_to_all x1, waiting for transfers between devices, body(): lax.all_to_all(query_up.reshape(query_up.shape[0], seq_count, heads * (NO...  46.6 us
    all_gather x1, waiting for transfers between devices, body(): packed = lax.all_gather(packed, 'seq', axis=0, tiled=False)  29.2 us
    all_to_all x1, blocking collectives, body(): lax.all_to_all(head_output, 'seq', split_axis=0, concat_axis=1, tiled=True)  27.7 us
    reduce_scatter x1, waiting for transfers between devices, body(): lax.psum_scatter(partial, 'tp', scatter_dimension=0, tiled=True)  26.4 us
    all_to_all x1, waiting for transfers between devices, body(): lax.all_to_all(key_up.reshape(key_up.shape[0], seq_count, heads * NOPE),...  13.3 us
    psum x1, blocking collectives, body(): square_sums = lax.psum(jnp.sum(inputs * inputs, 1), 'tp')  11.4 us
    unnamed x38, local copies, waits for them, and re-layouts  9.38 us
  transfers between devices with their start and end apart: 7, of which 6 were waited for; matrix products, arithmetic and copies ran while one was open for 5% of the time, Pallas kernels for 0%

commit v1 on v0

--- a/solution.py
+++ b/solution.py
@@ -166,7 +166,19 @@
     )
     score_scale = (NOPE + ROPE) ** (-0.5)
     head_output = heads_attention(query, key_all, value, group_ids, score_scale, doc_most)
-    attended = lax.all_to_all(head_output, "seq", split_axis=0, concat_axis=1, tiled=True)
+    ways, here = (lax.axis_size("seq"), lax.axis_index("seq"))
+    width_2 = head_output.shape[0] // ways
+    shape = list(head_output.shape)
+    shape[0] = width_2
+    height = shape[1]
+    shape[1] = height * ways
+    full = jnp.zeros(shape, head_output.dtype)
+    for mask in range(ways):
+        part = lax.dynamic_slice_in_dim(head_output, (here ^ mask) * width_2, width_2, axis=0)
+        if mask:
+            part = lax.ppermute(part, "seq", [(d, d ^ mask) for d in range(ways)])
+        full = lax.dynamic_update_slice_in_dim(full, part, (here ^ mask) * height, axis=1)
+    attended = full
     return attended.reshape(tok_count, local_heads * VDIM)
 
 

time: 380 us -> 376 us (0.989)
  blocking collectives: 46.9 us -> 19.2 us
  waiting for transfers between devices: 251 us -> 267 us
  starting transfers between devices: 10.9 us -> 15.3 us
    all_to_all x1 -> x0, blocking collectives: 27.7 us -> none  [body(): lax.all_to_all(head_output, 'seq', split_axis=0, concat_axis=1, tiled=True)]
    ppermute x0 -> x3, waiting for transfers between devices: none -> 16.8 us  [body(): part = lax.ppermute(part, 'seq', [(d, d ^ mask) for d in range(ways)])]
    all_to_all x1, waiting for transfers between devices: 13.3 us -> 8.32 us  [body(): lax.all_to_all(key_up.reshape(key_up.shape[0], seq_count, heads * NOPE),...]
    all_to_all x1, waiting for transfers between devices: 8.31 us -> 13.2 us  [body(): lax.all_to_all(value_up.reshape(value_up.shape[0], seq_count, heads * VDI...]
    ppermute x0 -> x3, starting transfers between devices: none -> 4.44 us  [body(): part = lax.ppermute(part, 'seq', [(d, d ^ mask) for d in range(ways)])]
    unnamed x38 -> x43, local copies, waits for them, and re-layouts: 9.38 us -> 9.89 us
  transfers between devices with their start and end apart: 7 -> 10, of which waited for: 6 -> 8; matrix products, arithmetic and copies ran while one was open for 5% -> 5% of each run, Pallas kernels for 0% -> 0%
where the time goes in v1:
time: 376 us; the launch traced here: 375 us
  waiting for transfers between devices  267 us (71%)
  local copies, waits for them, and re-layouts  27.4 us (7%)
  matrix products  20.3 us (5%)
  blocking collectives  19.2 us (5%)
  starting transfers between devices  15.3 us (4%)
  between operations  13.6 us (4%)
  other arithmetic  12.2 us (3%)
    all_gather x1, waiting for transfers between devices, body(): down_all = lax.all_gather(down_piece, 'seq', axis=1, tiled=True)  127 us
    all_to_all x1, waiting for transfers between devices, body(): lax.all_to_all(query_up.reshape(query_up.shape[0], seq_count, heads * (NO...  45.8 us
    all_gather x1, waiting for transfers between devices, body(): packed = lax.all_gather(packed, 'seq', axis=0, tiled=False)  29.2 us
    reduce_scatter x1, waiting for transfers between devices, body(): lax.psum_scatter(partial, 'tp', scatter_dimension=0, tiled=True)  26.4 us
    ppermute x3, waiting for transfers between devices, body(): part = lax.ppermute(part, 'seq', [(d, d ^ mask) for d in range(ways)])  16.8 us
    all_to_all x1, waiting for transfers between devices, body(): lax.all_to_all(value_up.reshape(value_up.shape[0], seq_count, heads * VDI...  13.2 us
    psum x1, blocking collectives, body(): square_sums = lax.psum(jnp.sum(inputs * inputs, 1), 'tp')  11.4 us
    unnamed x43, local copies, waits for them, and re-layouts  9.89 us
  transfers between devices with their start and end apart: 10, of which 8 were waited for; matrix products, arithmetic and copies ran while one was open for 5% of the time, Pallas kernels for 0%

profile of v1, /device:TPU:0, one launch (start us, length us, event | category | flops | bytes accessed | tf_op | source)
XLA Modules:
  0.0 375.2 jit_solution(16413752873503942649)
XLA Ops:
  6.5 1.8 copy.72
  8.4 2.6 pad_maximum_fusion
  11.3 11.4 %psum.7 = f32[256]{0:T(256)S(1)} all-reduce(f32[256]{0:T(256)S(1)} %fusion.16), channel_id=1, replica_groups=mesh['seq'=4,'tp'=4,'dp'=2] {'tp'}, use_global_device_ids=true, to_apply=%region_1.2 | all-reduce | flops 256 | bytes 2048 | tf_op jit(solution)/shard_map/psum | solution.py:100
  22.7 127.4 %all-gather.7.cloned.1.call-done = bf16[1792,2112]{0,1:T(8,128)(2,1)} async-done(((bf16[1792,528]{0,1:T(8,128)(2,1)}), bf16[1792,2112]{0,1:T(8,128)(2,1)}) %all-gather.7.cloned.1.call-update) | async-done | bytes 7569424 | tf_op jit(solution)/shard_map/all_gather | solution.py:105
  150.1 6.9 %fusion.33 = f32[256,2112]{1,0:T(8,128)} fusion(bf16[1792,2112]{0,1:T(8,128)(2,1)} %all-gather.7.cloned.1.call-done, bf16[256,1792]{1,0:T(8,128)(2,1)S(1)} %copy-done.5, f32[1792]{0:T(1024)S(1)} %copy-done.16, f32[256]{0:T(256)S(1)} %add_rsqrt_fusion), kind=kOutput, calls=%fused_computation.51 | convolution fusion | flops 1939603456 | bytes 10657792 | tf_op jit(solution)/shard_map/dot_general | solution.py:106
  157.1 7.9 %all-gather.2 = s32[4,1,256]{2,1,0:T(1,128)S(1)} all-gather(s32[1,1,256]{2,1,0:T(1,128)S(1)} %bitcast.84), channel_id=1, replica_groups=mesh['seq'=4,'tp'=4,'dp'=2] {'seq'}, dimensions={0}, use_global_device_ids=true | all-gather | bytes 5120 | tf_op jit(solution)/shard_map/all_gather | solution.py:94
  165.3 26.4 %reduce-scatter.2.cloned.1.call-done = f32[64,2112]{1,0:T(8,128)} async-done(((f32[256,2112]{1,0:T(8,128)}), f32[64,2112]{1,0:T(8,128)}) %reduce-scatter.2.cloned.1.call-update) | async-done | bytes 540688 | tf_op jit(solution)/shard_map/reduce_scatter | solution.py:107
  191.7 1.5 reshape.260
  195.7 29.2 %all-gather.9.cloned.1.call-done = bf16[256,2112]{1,0:T(8,128)(2,1)} async-done(((bf16[64,2112]{1,0:T(8,128)(2,1)}), bf16[256,2112]{1,0:T(8,128)(2,1)}) %all-gather.9.cloned.1.call-update) | async-done | bytes 1081360 | tf_op jit(solution)/shard_map/all_gather | solution.py:119
  225.9 3.5 all-to-all-start
  230.4 13.2 %all-to-all-done = bf16[128,4,512]{0,2,1:T(8,128)(2,1)S(1)} async-done(((bf16[128,4,512]{0,2,1:T(8,128)(2,1)}), bf16[128,4,512]{0,2,1:T(8,128)(2,1)S(1)}, u32[]{:S(2)}, u32[]{:S(2)}) %all-to-all-start) | async-done | bytes 524320 | tf_op jit(solution)/shard_map/all_to_all | solution.py:141
  243.7 3.5 all-to-all-start.2
  247.1 3.0 copy.80
  250.1 2.7 copy.81
  252.8 8.3 %all-to-all-done.2 = bf16[128,4,512]{0,2,1:T(8,128)(2,1)S(1)} async-done(((bf16[128,4,512]{0,2,1:T(8,128)(2,1)}), bf16[128,4,512]{0,2,1:T(8,128)(2,1)S(1)}, u32[]{:S(2)}, u32[]{:S(2)}) %all-to-all-start.2) | async-done | bytes 524320 | tf_op jit(solution)/shard_map/all_to_all | solution.py:134
  261.1 3.8 %all-to-all-start.1 = ((bf16[384,4,768]{2,0,1:T(8,128)(2,1)}), bf16[384,4,768]{2,0,1:T(8,128)(2,1)S(1)}, u32[]{:S(2)}, u32[]{:S(2)}) async-start(bf16[384,4,768]{2,0,1:T(8,128)(2,1)} %copy.81), calls=%async_computation.2 | async-start | bytes 4718592 | tf_op jit(solution)/shard_map/all_to_all | solution.py:127
  265.6 1.8 multiply_cosine_fusion
  268.4 1.8 compare_and_fusion
  272.3 45.8 %all-to-all-done.1 = bf16[384,4,768]{2,0,1:T(8,128)(2,1)S(1)} async-done(((bf16[384,4,768]{2,0,1:T(8,128)(2,1)}), bf16[384,4,768]{2,0,1:T(8,128)(2,1)S(1)}, u32[]{:S(2)}, u32[]{:S(2)}) %all-to-all-start.1) | async-done | bytes 2359328 | tf_op jit(solution)/shard_map/all_to_all | solution.py:127
  318.1 2.5 copy.82
  320.6 2.7 copy.77
  325.4 1.7 convolution_convert_fusion
  327.1 1.7 copy.85
  328.9 4.5 %fusion.6 = f32[1024,4,192]{0,2,1:T(8,128)S(1)} fusion(bf16[4,192,1536]{2,1,0:T(8,128)(2,1)S(1)} %bitcast.68, bf16[1024,2112]{1,0:T(8,128)(2,1)} %bitcast.62), kind=kOutput, calls=%fused_computation.11 | convolution fusion | flops 2415919104 | bytes 8650752 | tf_op jit(solution)/shard_map/dot_general | solution.py:148
  336.0 1.7 fusion
  338.7 1.3 divide_convert_fusion.1
  340.1 1.7 fusion.1
  341.8 2.3 divide_convert_fusion
  344.7 2.0 collective-permute-start.1
  346.7 2.4 collective-permute-start.2
  349.1 7.9 %collective-permute-done = bf16[256,4,128]{0,2,1:T(8,128)(2,1)S(1)} collective-permute-done((bf16[256,4,128]{0,2,1:T(8,128)(2,1)S(1)}, bf16[256,4,128]{0,2,1:T(8,128)(2,1)S(1)}, u32[]{:S(2)}, u32[]{:S(2)}) %collective-permute-start) | collective-permute-done | bytes 262176 | tf_op jit(solution)/shard_map/ppermute | solution.py:179
  357.0 8.9 %collective-permute-done.1 = bf16[256,4,128]{0,2,1:T(8,128)(2,1)S(1)} collective-permute-done((bf16[256,4,128]{0,2,1:T(8,128)(2,1)S(1)}, bf16[256,4,128]{0,2,1:T(8,128)(2,1)S(1)}, u32[]{:S(2)}, u32[]{:S(2)}) %collective-permute-start.1) | collective-permute-done | bytes 262176 | tf_op jit(solution)/shard_map/ppermute | solution.py:179
  (101 shorter events, 17.9 us)
Async XLA Ops:
  6.5 143.5 %all-gather.7.cloned.1.call-start = ((), (), s32[]{:S(2)}) async-start(), calls=%async_computation.4 | async-start | bytes 9461760 | tf_op jit(solution)/shard_map/all_gather | solution.py:105
  8.3 2.7 copy-start.5
  8.4 141.7 %copy-start.16 = (f32[1792]{0:T(1024)S(1)}, f32[1792]{0:T(1024)}, u32[]{:S(2)}) copy-start(f32[1792]{0:T(1024)} %param.11) | copy-start | bytes 21508
  11.0 180.7 %reduce-scatter.2.cloned.1.call-start = ((), (), s32[]{:S(2)}) async-start(), calls=%async_computation.5 | async-start | bytes 2785280 | tf_op jit(solution)/shard_map/reduce_scatter | solution.py:107
  22.7 134.4 %copy-start.15 = (s32[256]{0:T(256)S(1)}, s32[256]{0:T(256)}, u32[]{:S(2)}) copy-start(s32[256]{0:T(256)} %param.19) | copy-start | bytes 3076
  157.0 37.1 %copy-start.13 = (f32[512]{0:T(512)S(1)}, f32[512]{0:T(512)}, u32[]{:S(2)}) copy-start(f32[512]{0:T(512)} %param.15) | copy-start | bytes 6148
  157.0 37.7 %copy-start.12 = (f32[1536]{0:T(1024)S(1)}, f32[1536]{0:T(1024)}, u32[]{:S(2)}) copy-start(f32[1536]{0:T(1024)} %param.14) | copy-start | bytes 18436
  157.0 67.8 %all-gather.9.cloned.1.call-start = ((), (), s32[]{:S(2)}) async-start(), calls=%async_computation.6 | async-start | bytes 1392640 | tf_op jit(solution)/shard_map/all_gather | solution.py:119
  165.0 30.7 %copy-start.14 = (f32[32]{0:T(128)}, f32[32]{0:T(128)S(1)}, u32[]{:S(2)}) copy-start(f32[32]{0:T(128)S(1)} %multiply_power_fusion) | copy-start | bytes 388
  193.2 31.7 %copy-start.8 = (bf16[128,2048]{1,0:T(8,128)(2,1)S(1)}, bf16[128,2048]{1,0:T(8,128)(2,1)}, u32[]{:S(2)}) copy-start(bf16[128,2048]{1,0:T(8,128)(2,1)} %param.18) | copy-start | bytes 1572868
  193.8 35.6 %copy-start.9 = (bf16[128,2048]{1,0:T(8,128)(2,1)S(1)}, bf16[128,2048]{1,0:T(8,128)(2,1)}, u32[]{:S(2)}) copy-start(bf16[128,2048]{1,0:T(8,128)(2,1)} %param.17) | copy-start | bytes 1572868
  195.7 124.9 %all-gather.11.cloned.1.call-start = ((), (), s32[]{:S(2)}) async-start(), calls=%async_computation.7 | async-start | bytes 5570560 | tf_op jit(solution)/shard_map/all_gather | solution.py:120
  225.9 17.7 %all-to-all-start = ((bf16[128,4,512]{0,2,1:T(8,128)(2,1)}), bf16[128,4,512]{0,2,1:T(8,128)(2,1)S(1)}, u32[]{:S(2)}, u32[]{:S(2)}) async-start(bf16[128,4,512]{0,2,1:T(8,128)(2,1)} %bitcast.7), calls=%async_computation.1 | async-start | bytes 1048576 | tf_op jit(solution)/shard_map/all_to_all | solution.py:141
  243.7 17.5 %all-to-all-start.2 = ((bf16[128,4,512]{0,2,1:T(8,128)(2,1)}), bf16[128,4,512]{0,2,1:T(8,128)(2,1)S(1)}, u32[]{:S(2)}, u32[]{:S(2)}) async-start(bf16[128,4,512]{0,2,1:T(8,128)(2,1)} %bitcast.20), calls=%async_computation.3 | async-start | bytes 1048576 | tf_op jit(solution)/shard_map/all_to_all | solution.py:134
  261.1 57.0 %all-to-all-start.1 = ((bf16[384,4,768]{2,0,1:T(8,128)(2,1)}), bf16[384,4,768]{2,0,1:T(8,128)(2,1)S(1)}, u32[]{:S(2)}, u32[]{:S(2)}) async-start(bf16[384,4,768]{2,0,1:T(8,128)(2,1)} %copy.81), calls=%async_computation.2 | async-start | bytes 4718592 | tf_op jit(solution)/shard_map/all_to_all | solution.py:127
  320.6 3.5 copy-start.11
  323.3 2.1 copy-start
  323.3 2.1 copy-start.10
  324.8 8.6 %copy-start.2 = (bf16[1024,512]{0,1:T(8,128)(2,1)}, bf16[1024,512]{0,1:T(8,128)(2,1)S(1)}, u32[]{:S(2)}) copy-start(bf16[1024,512]{0,1:T(8,128)(2,1)S(1)} %convolution_convert_fusion.1) | copy-start | bytes 3145732
  324.8 4.1 %copy-start.1 = (bf16[1536,768]{0,1:T(8,128)(2,1)S(1)}, bf16[1536,768]{0,1:T(8,128)(2,1)}, u32[]{:S(2)}) copy-start(bf16[1536,768]{0,1:T(8,128)(2,1)} %copy.82) | copy-start | bytes 7077892
  328.9 4.8 %copy-start.6 = (f32[1024,32]{0,1:T(8,128)S(1)}, f32[1024,32]{0,1:T(8,128)}, u32[]{:S(2)}) copy-start(f32[1024,32]{0,1:T(8,128)} %get-tuple-element.16) | copy-start | bytes 393220
  333.4 0.9 copy-start.7
  333.6 1.0 copy-start.4
  333.6 1.3 copy-start.17
  334.9 1.0 copy-start.3
  337.7 1.0 slice-start
  340.0 1.7 slice-start.1
  344.7 12.3 %collective-permute-start = (bf16[256,4,128]{0,2,1:T(8,128)(2,1)S(1)}, bf16[256,4,128]{0,2,1:T(8,128)(2,1)S(1)}, u32[]{:S(2)}, u32[]{:S(2)}) collective-permute-start(bf16[256,4,128]{0,2,1:T(8,128)(2,1)S(1)} %get-tuple-element.9), channel_id=1, source_target_pairs={{0,8},{8,0},{16,24},{24,16},{1,9},{9,1},{17,25},{25,17},{2,10},{10... | collective-permute-start | bytes 786440 | tf_op jit(solution)/shard_map/ppermute | solution.py:179
  344.7 21.2 %collective-permute-start.1 = (bf16[256,4,128]{0,2,1:T(8,128)(2,1)S(1)}, bf16[256,4,128]{0,2,1:T(8,128)(2,1)S(1)}, u32[]{:S(2)}, u32[]{:S(2)}) collective-permute-start(bf16[256,4,128]{0,2,1:T(8,128)(2,1)S(1)} %get-tuple-element.10), channel_id=1, source_target_pairs={{0,16},{8,24},{16,0},{24,8},{1,17},{9,25},{17,1},{25,9},{2,18},{10... | collective-permute-start | bytes 786440 | tf_op jit(solution)/shard_map/ppermute | solution.py:179
  346.7 20.3 %collective-permute-start.2 = (bf16[256,4,128]{0,2,1:T(8,128)(2,1)S(1)}, bf16[256,4,128]{0,2,1:T(8,128)(2,1)S(1)}, u32[]{:S(2)}, u32[]{:S(2)}) collective-permute-start(bf16[256,4,128]{0,2,1:T(8,128)(2,1)S(1)} %get-tuple-element.7), channel_id=1, source_target_pairs={{0,24},{8,16},{16,8},{24,0},{1,25},{9,17},{17,9},{25,1},{2,26},{10... | collective-permute-start | bytes 786440 | tf_op jit(solution)/shard_map/ppermute | solution.py:179
Sparse Core Ops, SparseCore 0:
  11.1 138.9 all-gather.6
  157.2 34.4 reduce-scatter.1
  195.8 29.0 all-gather.8
  226.6 54.1 all-gather.10
